TPU v7x, 128 devices: a whole 4x4x4 slice. The times are simulated.
128 devices in a mesh: req: 4 (over z), vocab: 32 (over y, x, core).
Axes of the slice: x: 4, y: 4, z: 4, core: 2. Of those that a mesh axis runs over, the one named last changes fastest.
Arguments:
- hidden: bfloat16 [16, 1536, 2048], P('req', 'vocab'), may hold values from -80 to 80
- norm_gain: float32 [2048], replicated, may hold values from 0.6 to 1.4
- head_weight: bfloat16 [2048, 32000], P(None, 'vocab'), may hold values from -2 to 2
- token_ids: int32 [16, 1536], P('req', 'vocab'), may hold values from 0 to 31999
- lengths: int32 [16], replicated, may hold values from 1 to 1536, 15360 in all
- group_ids: int32 [16], replicated, may hold values from 0 to 3
Outputs:
- logprob: float32 [16, 1536], P('req', 'vocab')
- entropy: float32 [16, 1536], P('req', 'vocab')
- centered: float32 [16], replicated
Inputs may be any that keep to these rules, and one draw needn't show every extreme that they name: The lengths sum to 15360; the longest is 1536.
All inputs are finite; a program needn't handle non-finite values.
Results may differ from a plain program's by a relative error of at most 0.00093.
Values may be sent and summed in bfloat16 or wider, within the bound.
No kernel may reach another device: no remote copies, remote signals or barrier semaphores. Data moves between devices by JAX's collectives and lax.ppermute only.
A program may use at most 128 MiB of HBM per device.

v0:
```python
import jax
import jax.numpy as jnp
from jax import lax
from jax.sharding import PartitionSpec as P

norm_eps = 1e-06


def slice_stats(rows, tokens, weight, offset):
    row_count = rows.shape[0]
    block_len = min(512, row_count)
    columns = jnp.arange(weight.shape[1], dtype=jnp.int32)
    results = []
    for block_start in range(0, row_count, block_len):
        block_rows = rows[block_start : block_start + block_len]
        local_ids = tokens[block_start : block_start + block_len] - offset
        logits = jnp.dot(block_rows, weight, preferred_element_type=jnp.float32)
        row_top = jnp.max(logits, axis=1)
        exps = jnp.exp(logits - row_top[:, None])
        exp_total = jnp.sum(exps, axis=1)
        moment = jnp.sum(exps * logits, axis=1)
        picked = jnp.sum(jnp.where(columns[None, :] == local_ids[:, None], logits, 0.0), axis=1)
        results.append((row_top, exp_total, moment, picked))
    return tuple((jnp.concatenate([item[slot] for item in results]) for slot in range(4)))


def body(hidden, norm_gain, head_weight, token_ids, lengths, group_ids):
    req_dev, pos_dev, model_width = hidden.shape
    vocab_dev = head_weight.shape[1]
    vocab_index = lax.axis_index("vocab")
    req_index = lax.axis_index("req")
    values = hidden.astype(jnp.float32)
    squares = jnp.mean(values * values, axis=-1, keepdims=True)
    normed = (values * lax.rsqrt(squares + norm_eps) * norm_gain).astype(jnp.bfloat16)
    own_rows = req_dev * pos_dev
    flat_rows = normed.reshape(own_rows, model_width)
    flat_tokens = token_ids.reshape(own_rows)
    offset = vocab_index * vocab_dev
    fresh = slice_stats(
        lax.all_gather(flat_rows, "vocab", axis=0, tiled=True),
        lax.all_gather(flat_tokens, "vocab", axis=0, tiled=True),
        head_weight,
        offset,
    )
    maxima, sums, moments, picked = tuple((new_part for new_part in fresh))
    own_start = vocab_index * own_rows
    row_top = lax.pmax(maxima, "vocab")
    rescale = jnp.exp(maxima - row_top)
    exp_total, moment, token_logit = lax.psum((sums * rescale, moments * rescale, picked), "vocab")
    row_top = lax.dynamic_slice_in_dim(row_top, own_start, own_rows)
    exp_total = lax.dynamic_slice_in_dim(exp_total, own_start, own_rows)
    moment = lax.dynamic_slice_in_dim(moment, own_start, own_rows)
    token_logit = lax.dynamic_slice_in_dim(token_logit, own_start, own_rows)
    log_total = row_top + jnp.log(exp_total)
    raw_logprob = (token_logit - log_total).reshape(req_dev, pos_dev)
    raw_entropy = (log_total - moment / exp_total).reshape(req_dev, pos_dev)
    positions = vocab_index * pos_dev + jnp.arange(pos_dev, dtype=jnp.int32)
    own_lengths = lax.dynamic_slice_in_dim(lengths, req_index * req_dev, req_dev)
    is_live = positions[None, :] < own_lengths[:, None]
    logprob = jnp.where(is_live, raw_logprob, 0.0)
    entropy = jnp.where(is_live, raw_entropy, 0.0)
    partial_sums = jnp.sum(logprob, axis=1)
    request_count = lengths.shape[0]
    global_rows = req_index * req_dev + jnp.arange(req_dev, dtype=jnp.int32)
    slots = jnp.arange(request_count, dtype=jnp.int32)
    placed = jnp.sum(
        jnp.where(slots[None, :] == global_rows[:, None], partial_sums[:, None], 0.0), axis=0
    )
    seq_sum = lax.psum(placed, ("req", "vocab"))
    same = (group_ids[:, None] == group_ids[None, :]).astype(jnp.float32)
    members = jnp.sum(same, axis=1)
    group_mean = jnp.sum(same * seq_sum[None, :], axis=1) / members
    spread = jnp.sum(same * (seq_sum[None, :] - group_mean[:, None]) ** 2, axis=1) / members
    group_std = jnp.maximum(jnp.sqrt(spread), 1.0)
    centered = (seq_sum - group_mean) / group_std
    return (logprob, entropy, centered)


def solution(mesh):
    return jax.shard_map(
        body,
        mesh=mesh,
        in_specs=(P("req", "vocab", None), P(), P(None, "vocab"), P("req", "vocab"), P(), P()),
        out_specs=(P("req", "vocab"), P("req", "vocab"), P()),
        check_vma=False,
    )
```

profile of v0, /device:TPU:2, one launch (start us, length us, event | category | flops | bytes accessed | tf_op | source)
XLA Modules:
  0.0 503.8 jit_solution(15608291727772157882)
XLA Ops:
  7.2 0.0 copy-start.15
  7.2 0.0 copy-start.11
  7.2 0.0 all-gather.2.cloned.1.call-start
  7.2 1.4 fusion.36
  8.6 2.3 fusion.38
  10.9 0.0 all-gather.2.cloned.1.call-update
  11.0 0.0 all-reduce.4.cloned.1.call-start
  11.1 0.0 copy-done.11
  11.1 0.1 reshape.73
  11.2 0.0 copy-done.15
  11.2 0.6 dynamic-slice
  12.4 0.3 dynamic-update-slice
  12.7 126.6 %all-reduce = s32[6144]{0:T(1024)S(1)} all-reduce(s32[6144]{0:T(1024)S(1)} %dynamic-update-slice), channel_id=1, replica_groups=mesh['req'=4,'vocab'=32] {'vocab'}, use_global_device_ids=true, to_apply=%add | all-reduce | flops 6144 | bytes 49152
  139.3 0.0 all-gather.2.cloned.1.call-done
  139.3 0.0 copy-start.12
  139.3 6.6 %fusion.45 = (f32[512]{0:T(512)S(1)}, f32[512,1000]{0,1:T(8,128)}) fusion(bf16[2048,1000]{0,1:T(8,128)(2,1)} %param.8, bf16[6144,2048]{1,0:T(8,128)(2,1)} %all-gather.2.cloned.1.call-done), kind=kOutput, calls=%fused_computation.170 | convolution fusion | flops 2097663488 | bytes 8243200 | tf_op jit(solution)/shard_map/dot_general | solution.py:17
  146.0 4.1 copy-done.12
  150.1 5.9 %fusion.46 = (f32[512]{0:T(512)S(1)}, f32[512,1000]{0,1:T(8,128)}) fusion(bf16[2048,1000]{0,1:T(8,128)(2,1)} %param.8, bf16[6144,2048]{1,0:T(8,128)(2,1)S(1)} %copy-done.12), kind=kOutput, calls=%fused_computation.171 | convolution fusion | flops 2097663488 | bytes 8243200 | tf_op jit(solution)/shard_map/dot_general | solution.py:17
  156.0 0.0 copy-done.13
  156.0 3.6 fusion.47
  159.7 3.6 fusion.48
  163.3 3.7 fusion.49
  167.0 3.6 fusion.50
  170.6 3.8 fusion.51
  174.4 3.6 fusion.52
  178.0 3.6 fusion.53
  181.7 3.6 fusion.54
  185.3 2.3 fusion.55
  187.6 3.6 fusion.56
  191.2 124.0 %pmax.7 = f32[6144]{0:T(1024)S(1)} all-reduce(f32[6144]{0:T(1024)S(1)} %constant_dynamic-update-slice_fusion.1), channel_id=1, replica_groups=mesh['req'=4,'vocab'=32] {'vocab'}, use_global_device_ids=true, to_apply=%region_26.27 | all-reduce | flops 6144 | bytes 49152 | tf_op jit(solution)/shard_map/pmax | solution.py:47
  315.2 3.7 multiply_reduce_fusion.10
  318.9 0.0 copy-done.7
  318.9 0.0 copy-done.8
  318.9 0.0 copy-start.5
  318.9 0.0 copy-start.6
  319.0 1.3 multiply_reduce_fusion.8
  320.3 0.2 copy-done.5
  320.5 0.6 copy-done.6
  321.1 1.3 multiply_reduce_fusion.6
  322.5 0.2 copy-done.3
  322.7 0.6 copy-done.4
  323.3 1.3 multiply_reduce_fusion.4
  324.7 0.2 copy-done.1
  324.9 0.6 copy-done.2
  325.5 1.3 multiply_reduce_fusion.2
  326.9 0.2 copy-done
  327.1 1.3 multiply_reduce_fusion
  328.8 0.0 copy-start.9
  328.8 0.6 fusion.39
  329.4 0.0 copy-done.9
  329.4 0.0 all-reduce.4.cloned.1.call-update
  329.4 0.0 copy-done.14
  329.4 0.1 dynamic_slice.15
  329.5 99.0 %all-reduce.4.cloned.1.call-done = (f32[6144]{0:T(1024)}, f32[6144]{0:T(1024)}, f32[6144]{0:T(1024)}) async-done(((f32[6144]{0:T(1024)}, f32[6144]{0:T(1024)}, f32[6144]{0:T(1024)}), (f32[6144]{0:T(1024)}, f32[6144]{0:T(1024)}, f32[6144]{0:T(1024)})) %all-reduce.4.cloned.1.call-update) | async-done | bytes 73744 | tf_op jit(solution)/shard_map/psum | solution.py:49
  428.5 0.8 divide_subtract_fusion
  429.3 0.1 reshape.71
  429.4 0.1 reshape.72
  429.5 0.8 fusion.44
  430.2 0.1 select_reduce_fusion.12
  430.3 65.7 %psum.31 = f32[16]{0:T(128)S(1)} all-reduce(f32[16]{0:T(128)S(1)} %select_reduce_fusion.12), channel_id=1, replica_groups=mesh['req'=4,'vocab'=32] {'req','vocab'}, use_global_device_ids=true, to_apply=%region_55.56 | all-reduce | flops 16 | bytes 128 | tf_op jit(solution)/shard_map/psum | solution.py:69
  496.1 0.0 copy-done.10
  496.1 0.2 fusion.42
  496.3 0.2 fusion.43
  496.4 0.5 maximum_divide_fusion
  (68 shorter events, 0.3 us)
Async XLA Ops:
  7.2 4.0 copy-start.15
  7.2 3.9 copy-start.11
  7.2 132.1 %all-gather.2.cloned.1.call-start = ((), (), s32[]{:S(2)}) async-start(), calls=%async_computation | async-start | bytes 25952256 | tf_op jit(solution)/shard_map/all_gather | solution.py:40
  11.0 417.5 %all-reduce.4.cloned.1.call-start = ((), (), s32[]{:S(2)}) async-start(), calls=%async_computation.1 | async-start | bytes 147456 | tf_op jit(solution)/shard_map/psum | solution.py:49
  139.3 10.7 %copy-start.12 = (bf16[6144,2048]{1,0:T(8,128)(2,1)S(1)}, bf16[6144,2048]{1,0:T(8,128)(2,1)}, u32[]{:S(2)}) copy-start(bf16[6144,2048]{1,0:T(8,128)(2,1)} %all-gather.2.cloned.1.call-done) | copy-start | bytes 75497472
  150.1 6.0 %copy-start.13 = (bf16[2048,1000]{0,1:T(8,128)(2,1)S(1)}, bf16[2048,1000]{0,1:T(8,128)(2,1)}, u32[]{:S(2)}) copy-start(bf16[2048,1000]{0,1:T(8,128)(2,1)} %param.8) | copy-start | bytes 12288004
  315.2 3.7 copy-start.7
  315.2 3.7 copy-start.8
  318.9 1.6 copy-start.5
  318.9 2.2 copy-start.6
  321.1 1.6 copy-start.3
  321.1 2.2 copy-start.4
  323.3 1.6 copy-start.1
  323.3 2.2 copy-start.2
  325.5 1.6 copy-start
  327.1 2.4 copy-start.14
  327.1 169.0 %copy-start.10 = (s32[16]{0:T(128)S(1)}, s32[16]{0:T(128)}, u32[]{:S(2)}) copy-start(s32[16]{0:T(128)} %param.11) | copy-start | bytes 196
  328.8 0.6 copy-start.9
Sparse Core Ops, SparseCore 0:
  11.1 94.1 all-gather.1
  329.5 98.8 all-reduce.3
where the time goes:
time: 505 us; the launch traced here: 504 us
  blocking collectives  316 us (63%)
  waiting for transfers between devices  99 us (20%)
  matrix products  47.7 us (9%)
  other arithmetic  17.3 us (3%)
  between operations  15.1 us (3%)
  local copies, waits for them, and re-layouts  8.28 us (2%)
    unnamed x1, blocking collectives  127 us
    pmax x1, blocking collectives, body(): row_top = lax.pmax(maxima, 'vocab')  124 us
    psum x1, waiting for transfers between devices, body(): lax.psum((sums * rescale, moments * rescale, picked), 'vocab')  99 us
    psum x1, blocking collectives, body(): seq_sum = lax.psum(placed, ('req', 'vocab'))  65.7 us
    dot_general x12, matrix products, slice_stats(): logits = jnp.dot(block_rows, weight, preferred_element_type=jnp.float32)  47.7 us
    reduce_sum x6, other arithmetic, slice_stats(): moment = jnp.sum(exps * logits, axis=1)  10.3 us
  transfers between devices with their start and end apart: 2, of which 1 were waited for; matrix products, arithmetic and copies ran while one was open for 0% of the time, Pallas kernels for 0%

commit v1 on v0

v1 whole, which is shorter than its diff:
```python
import jax
import jax.numpy as jnp
from jax import lax
from jax.sharding import PartitionSpec as P

norm_eps = 1e-06
OFFLOAD_FLOATS = 8192


def slice_stats(rows, tokens, weight, offset):
    row_count = rows.shape[0]
    block_len = min(512, row_count)
    columns = jnp.arange(weight.shape[1], dtype=jnp.int32)
    results = []
    for block_start in range(0, row_count, block_len):
        block_rows = rows[block_start : block_start + block_len]
        local_ids = tokens[block_start : block_start + block_len] - offset
        logits = jnp.dot(block_rows, weight, preferred_element_type=jnp.float32)
        row_top = jnp.max(logits, axis=1)
        exps = jnp.exp(logits - row_top[:, None])
        exp_total = jnp.sum(exps, axis=1)
        moment = jnp.sum(exps * logits, axis=1)
        picked = jnp.sum(jnp.where(columns[None, :] == local_ids[:, None], logits, 0.0), axis=1)
        results.append(jnp.stack([row_top, exp_total, moment, picked]))
    return jnp.concatenate(results, axis=1)


def combine(stats):
    maxima, sums, moments, picked = stats[:, 0], stats[:, 1], stats[:, 2], stats[:, 3]
    row_top = jnp.max(maxima, axis=0)
    rescale = jnp.exp(maxima - row_top[None, :])
    exp_total = jnp.sum(sums * rescale, axis=0)
    moment = jnp.sum(moments * rescale, axis=0)
    token_logit = jnp.sum(picked, axis=0)
    log_total = row_top + jnp.log(exp_total)
    return token_logit - log_total, log_total - moment / exp_total


def padded_gather(x, axis_name):
    n = x.shape[0]
    width = max(n, OFFLOAD_FLOATS)
    padded = jnp.zeros((1, width), jnp.float32).at[0, :n].set(x)
    return lax.all_gather(padded, axis_name, axis=0, tiled=True)[:, :n]


def body(hidden, norm_gain, head_weight, token_ids, lengths, group_ids):
    req_dev, pos_dev, model_width = hidden.shape
    vocab_dev = head_weight.shape[1]
    n_vocab = lax.axis_size("vocab")
    n_req = lax.axis_size("req")
    vocab_index = lax.axis_index("vocab")
    req_index = lax.axis_index("req")
    values = hidden.astype(jnp.float32)
    squares = jnp.mean(values * values, axis=-1, keepdims=True)
    normed = (values * lax.rsqrt(squares + norm_eps) * norm_gain).astype(jnp.bfloat16)
    offset = vocab_index * vocab_dev
    tok = padded_gather(token_ids.astype(jnp.float32).reshape(-1), "vocab")
    all_tokens = tok.reshape(n_vocab, req_dev, pos_dev).transpose(1, 0, 2).reshape(req_dev, n_vocab * pos_dev)
    all_tokens = all_tokens.astype(jnp.int32)
    full_len = all_tokens.shape[1]
    own_lengths = lax.dynamic_slice_in_dim(lengths, req_index * req_dev, req_dev)
    positions = jnp.arange(full_len, dtype=jnp.int32)
    logprobs, entropies, seq_parts = [], [], []
    for k in range(req_dev):
        rows = lax.all_gather(normed[k], "vocab", axis=0, tiled=True)
        part = slice_stats(rows, all_tokens[k], head_weight, offset)
        stats = padded_gather(part.reshape(-1), "vocab").reshape(n_vocab, 4, full_len)
        raw_logprob, raw_entropy = combine(stats)
        is_live = positions < own_lengths[k]
        logprob = jnp.where(is_live, raw_logprob, 0.0)
        entropy = jnp.where(is_live, raw_entropy, 0.0)
        seq_parts.append(jnp.sum(logprob))
        logprobs.append(lax.dynamic_slice_in_dim(logprob, vocab_index * pos_dev, pos_dev))
        entropies.append(lax.dynamic_slice_in_dim(entropy, vocab_index * pos_dev, pos_dev))
    own_seq = jnp.stack(seq_parts)
    slots = jnp.arange(n_req * req_dev, dtype=jnp.int32) // req_dev
    seq_sum = jnp.where(slots == req_index, jnp.tile(own_seq, n_req), 0.0)
    for shift in range(1, n_req):
        moved = lax.ppermute(own_seq, "req", [(i, (i + shift) % n_req) for i in range(n_req)])
        source = (req_index + n_req - shift) % n_req
        seq_sum = seq_sum + jnp.where(slots == source, jnp.tile(moved, n_req), 0.0)
    same = (group_ids[:, None] == group_ids[None, :]).astype(jnp.float32)
    members = jnp.sum(same, axis=1)
    group_mean = jnp.sum(same * seq_sum[None, :], axis=1) / members
    spread = jnp.sum(same * (seq_sum[None, :] - group_mean[:, None]) ** 2, axis=1) / members
    group_std = jnp.maximum(jnp.sqrt(spread), 1.0)
    centered = (seq_sum - group_mean) / group_std
    return (jnp.stack(logprobs), jnp.stack(entropies), centered)


def solution(mesh):
    return jax.shard_map(
        body,
        mesh=mesh,
        in_specs=(P("req", "vocab", None), P(), P(None, "vocab"), P("req", "vocab"), P(), P()),
        out_specs=(P("req", "vocab"), P("req", "vocab"), P()),
        check_vma=False,
    )
```

time: 505 us -> 469 us (0.929); the launches traced: 504 us -> 460 us
  blocking collectives: 316 us -> 0 us
  waiting for transfers between devices: 99 us -> 342 us
  other arithmetic: 17.3 us -> 38.9 us
  local copies, waits for them, and re-layouts: 8.28 us -> 17.8 us
  matrix products: 47.7 us -> 39.6 us
  starting transfers between devices: 0.08 us -> 6.94 us
    all_gather x1 -> x9, waiting for transfers between devices: 0.02 us -> 340 us  [the longest x5 184 us: padded_gather(): return lax.all_gather(padded, axis_name, axis=0, tiled=True)[:, :n]]
    unnamed x1 -> x0, blocking collectives: 127 us -> none
    pmax x1 -> x0, blocking collectives: 124 us -> none  [body(): row_top = lax.pmax(maxima, 'vocab')]
    psum x1 -> x0, waiting for transfers between devices: 99 us -> none  [body(): lax.psum((sums * rescale, moments * rescale, picked), 'vocab')]
    psum x1 -> x0, blocking collectives: 65.7 us -> none  [body(): seq_sum = lax.psum(placed, ('req', 'vocab'))]
    another operation x0 -> x10, other arithmetic: none -> 9.44 us  [the longest x6 4.23 us: body(): return (jnp.stack(logprobs), jnp.stack(entropies), centered)]
    dot_general x12, matrix products: 47.7 us -> 39.6 us  [slice_stats(): logits = jnp.dot(block_rows, weight, preferred_element_type=jnp.float32)]
    ppermute x0 -> x3, starting transfers between devices: none -> 5.79 us  [body(): lax.ppermute(own_seq, 'req', [(i, (i + shift) % n_req) for i in range(n_r...]
  transfers between devices with their start and end apart: 2 -> 12, of which waited for: 1 -> 9; matrix products, arithmetic and copies ran while one was open for 0% -> 18% of each run, Pallas kernels for 0% -> 0%
where the time goes in v1:
time: 469 us; the launch traced here: 460 us
  waiting for transfers between devices  342 us (73%)
  matrix products  39.6 us (8%)
  other arithmetic  38.9 us (8%)
  local copies, waits for them, and re-layouts  17.8 us (4%)
  between operations  14.6 us (3%)
  starting transfers between devices  6.94 us (1%)
    all_gather x5, waiting for transfers between devices, padded_gather(): return lax.all_gather(padded, axis_name, axis=0, tiled=True)[:, :n]  184 us
    all_gather x4, waiting for transfers between devices, body(): rows = lax.all_gather(normed[k], 'vocab', axis=0, tiled=True)  156 us
    dot_general x12, matrix products, slice_stats(): logits = jnp.dot(block_rows, weight, preferred_element_type=jnp.float32)  39.6 us
    unnamed x48, local copies, waits for them, and re-layouts  12.7 us
  transfers between devices with their start and end apart: 12, of which 9 were waited for; matrix products, arithmetic and copies ran while one was open for 18% of the time, Pallas kernels for 0%

profile of v1, /device:TPU:2, one launch (start us, length us, event | category | flops | bytes accessed | tf_op | source)
XLA Modules:
  0.0 460.0 jit_solution(11580479027307848466)
XLA Ops:
  7.8 1.3 convert_select_fusion
  10.0 1.4 fusion.24
  11.3 1.4 fusion.26
  12.7 0.9 fusion.66
  13.7 0.7 all-gather.19.cloned.1.call-update
  16.3 38.5 %all-gather.27.cloned.1.call-done = f32[32,1,8192]{2,1,0:T(1,128)} async-done(((f32[1,1,8192]{2,1,0:T(1,128)}), f32[32,1,8192]{2,1,0:T(1,128)}) %all-gather.27.cloned.1.call-update) | async-done | bytes 1048592 | tf_op jit(solution)/shard_map/all_gather | solution.py:43
  54.7 1.8 copy.146
  56.8 47.7 %all-gather.21.cloned.1.call-done = bf16[1,1536,2048]{2,1,0:T(8,128)(2,1)} async-done(((bf16[1,48,2048]{2,1,0:T(8,128)(2,1)}), bf16[1,1536,2048]{2,1,0:T(8,128)(2,1)}) %all-gather.21.cloned.1.call-update) | async-done | bytes 6291472 | tf_op jit(solution)/shard_map/all_gather | solution.py:65
  104.6 5.3 %fusion.79 = (f32[512]{0:T(512)S(1)}, f32[512,1000]{0,1:T(8,128)S(1)}) fusion(bf16[2048,1000]{0,1:T(8,128)(2,1)} %param.18, bf16[1,1536,2048]{2,1,0:T(8,128)(2,1)} %all-gather.21.cloned.1.call-done), kind=kOutput, calls=%fused_computation.235 | convolution fusion | flops 2097663488 | bytes 8243200 | tf_op jit(solution)/shard_map/dot_general | solution.py:18
  109.8 0.7 fusion.20
  110.5 2.3 fusion.78
  112.9 0.7 fusion.19
  113.5 2.3 fusion.77
  115.9 0.7 fusion.18
  116.5 0.7 fusion.48
  118.1 36.4 %all-gather.19.cloned.1.call-done = bf16[1,1536,2048]{2,1,0:T(8,128)(2,1)} async-done(((bf16[1,48,2048]{2,1,0:T(8,128)(2,1)}), bf16[1,1536,2048]{2,1,0:T(8,128)(2,1)}) %all-gather.19.cloned.1.call-update) | async-done | bytes 6291472 | tf_op jit(solution)/shard_map/all_gather | solution.py:65
  154.5 5.3 %fusion.81 = (f32[512]{0:T(512)S(1)}, f32[512,1000]{0,1:T(8,128)S(1)}) fusion(bf16[2048,1000]{0,1:T(8,128)(2,1)} %param.18, bf16[1,1536,2048]{2,1,0:T(8,128)(2,1)} %all-gather.19.cloned.1.call-done), kind=kOutput, calls=%fused_computation.237 | convolution fusion | flops 2097663488 | bytes 8243200 | tf_op jit(solution)/shard_map/dot_general | solution.py:18
  160.5 2.3 fusion.80
  162.8 0.7 fusion.21
  163.5 2.3 fusion.82
  165.8 0.7 fusion.23
  166.5 0.7 fusion.47
  168.3 36.0 %all-gather.25.cloned.1.call-done = bf16[1,1536,2048]{2,1,0:T(8,128)(2,1)} async-done(((bf16[1,48,2048]{2,1,0:T(8,128)(2,1)}), bf16[1,1536,2048]{2,1,0:T(8,128)(2,1)}) %all-gather.25.cloned.1.call-update) | async-done | bytes 6291472 | tf_op jit(solution)/shard_map/all_gather | solution.py:65
  204.4 5.3 %fusion.73 = (f32[512]{0:T(512)S(1)}, f32[512,1000]{0,1:T(8,128)S(1)}) fusion(bf16[2048,1000]{0,1:T(8,128)(2,1)} %param.18, bf16[1,1536,2048]{2,1,0:T(8,128)(2,1)} %all-gather.25.cloned.1.call-done), kind=kOutput, calls=%fused_computation.229 | convolution fusion | flops 2097663488 | bytes 8243200 | tf_op jit(solution)/shard_map/dot_general | solution.py:18
  209.6 0.7 fusion.14
  210.3 2.3 fusion.72
  213.3 2.3 fusion.71
  215.6 0.7 fusion.12
  216.3 0.7 fusion.50
  217.9 36.3 %all-gather.23.cloned.1.call-done = bf16[1,1536,2048]{2,1,0:T(8,128)(2,1)} async-done(((bf16[1,48,2048]{2,1,0:T(8,128)(2,1)}), bf16[1,1536,2048]{2,1,0:T(8,128)(2,1)}) %all-gather.23.cloned.1.call-update) | async-done | bytes 6291472 | tf_op jit(solution)/shard_map/all_gather | solution.py:65
  254.2 5.3 %fusion.76 = (f32[512]{0:T(512)S(1)}, f32[512,1000]{0,1:T(8,128)S(1)}) fusion(bf16[2048,1000]{0,1:T(8,128)(2,1)} %param.18, bf16[1,1536,2048]{2,1,0:T(8,128)(2,1)} %all-gather.23.cloned.1.call-done), kind=kOutput, calls=%fused_computation.232 | convolution fusion | flops 2097663488 | bytes 8243200 | tf_op jit(solution)/shard_map/dot_general | solution.py:18
  259.4 0.7 fusion.17
  260.1 2.3 fusion.75
  262.4 0.7 fusion.16
  263.1 2.3 fusion.74
  266.1 0.7 fusion.49
  267.6 0.7 fusion.70
  268.3 1.2 iota_compare_fusion.15
  269.5 1.3 iota_compare_fusion.14
  270.8 1.3 iota_compare_fusion.13
  272.1 1.2 iota_compare_fusion.12
  273.2 25.0 %all-gather.31.cloned.1.call-done = f32[32,1,8192]{2,1,0:T(1,128)} async-done(((f32[1,1,8192]{2,1,0:T(1,128)}), f32[32,1,8192]{2,1,0:T(1,128)}) %all-gather.31.cloned.1.call-update) | async-done | bytes 1048592 | tf_op jit(solution)/shard_map/all_gather | solution.py:43
  298.2 1.8 copy.144
  300.7 41.7 %all-gather.29.cloned.1.call-done = f32[32,1,8192]{2,1,0:T(1,128)} async-done(((f32[1,1,8192]{2,1,0:T(1,128)}), f32[32,1,8192]{2,1,0:T(1,128)}) %all-gather.29.cloned.1.call-update) | async-done | bytes 1048592 | tf_op jit(solution)/shard_map/all_gather | solution.py:43
  342.4 1.8 copy.145
  344.8 41.7 %all-gather.35.cloned.1.call-done = f32[32,1,8192]{2,1,0:T(1,128)} async-done(((f32[1,1,8192]{2,1,0:T(1,128)}), f32[32,1,8192]{2,1,0:T(1,128)}) %all-gather.35.cloned.1.call-update) | async-done | bytes 1048592 | tf_op jit(solution)/shard_map/all_gather | solution.py:43
  386.5 1.8 copy.142
  388.4 0.7 reshape.411
  389.1 1.2 fusion.67
  390.3 2.1 fusion.65
  392.4 1.2 fusion.69
  393.5 37.0 %all-gather.33.cloned.1.call-done = f32[32,1,8192]{2,1,0:T(1,128)} async-done(((f32[1,1,8192]{2,1,0:T(1,128)}), f32[32,1,8192]{2,1,0:T(1,128)}) %all-gather.33.cloned.1.call-update) | async-done | bytes 1048592 | tf_op jit(solution)/shard_map/all_gather | solution.py:43
  430.6 1.8 copy.143
  434.1 0.8 fusion.46
  434.9 2.0 fusion.61
  437.1 1.9 fusion.63
  439.0 2.6 pad_maximum_fusion.2
  441.6 1.6 collective-permute-start
  443.2 2.9 collective-permute-start.1
  446.0 1.4 collective-permute-start.2
  447.8 0.8 fusion.57
  448.6 0.8 fusion.58
  449.3 0.8 fusion.59
  450.1 0.8 fusion.60
  (106 shorter events, 14.9 us)
Async XLA Ops:
  7.2 47.6 %all-gather.27.cloned.1.call-start = ((), (), s32[]{:S(2)}) async-start(), calls=%async_computation.4 | async-start | bytes 1081344 | tf_op jit(solution)/shard_map/all_gather | solution.py:43
  9.9 94.7 %all-gather.21.cloned.1.call-start = ((), (), s32[]{:S(2)}) async-start(), calls=%async_computation.1 | async-start | bytes 6488064 | tf_op jit(solution)/shard_map/all_gather | solution.py:65
  13.7 140.9 %all-gather.19.cloned.1.call-start = ((), (), s32[]{:S(2)}) async-start(), calls=%async_computation | async-start | bytes 6488064 | tf_op jit(solution)/shard_map/all_gather | solution.py:65
  14.4 189.9 %all-gather.25.cloned.1.call-start = ((), (), s32[]{:S(2)}) async-start(), calls=%async_computation.3 | async-start | bytes 6488064 | tf_op jit(solution)/shard_map/all_gather | solution.py:65
  15.0 239.2 %all-gather.23.cloned.1.call-start = ((), (), s32[]{:S(2)}) async-start(), calls=%async_computation.2 | async-start | bytes 6488064 | tf_op jit(solution)/shard_map/all_gather | solution.py:65
  15.6 282.7 %all-gather.31.cloned.1.call-start = ((), (), s32[]{:S(2)}) async-start(), calls=%async_computation.6 | async-start | bytes 1081344 | tf_op jit(solution)/shard_map/all_gather | solution.py:43
  104.6 5.9 %copy-start.11 = (bf16[1,1536,2048]{2,1,0:T(8,128)(2,1)S(1)}, bf16[1,1536,2048]{2,1,0:T(8,128)(2,1)}, u32[]{:S(2)}) copy-start(bf16[1,1536,2048]{2,1,0:T(8,128)(2,1)} %all-gather.21.cloned.1.call-done) | copy-start | bytes 18874372
  104.6 6.0 %copy-start.12 = (bf16[2048,1000]{0,1:T(8,128)(2,1)S(1)}, bf16[2048,1000]{0,1:T(8,128)(2,1)}, u32[]{:S(2)}) copy-start(bf16[2048,1000]{0,1:T(8,128)(2,1)} %param.18) | copy-start | bytes 12288004
  117.9 224.5 %all-gather.29.cloned.1.call-start = ((), (), s32[]{:S(2)}) async-start(), calls=%async_computation.5 | async-start | bytes 1081344 | tf_op jit(solution)/shard_map/all_gather | solution.py:43
  154.5 5.9 %copy-start.10 = (bf16[1,1536,2048]{2,1,0:T(8,128)(2,1)S(1)}, bf16[1,1536,2048]{2,1,0:T(8,128)(2,1)}, u32[]{:S(2)}) copy-start(bf16[1,1536,2048]{2,1,0:T(8,128)(2,1)} %all-gather.19.cloned.1.call-done) | copy-start | bytes 18874372
  154.5 6.0 %copy-start.13 = (bf16[2048,1000]{0,1:T(8,128)(2,1)S(1)}, bf16[2048,1000]{0,1:T(8,128)(2,1)}, u32[]{:S(2)}) copy-start(bf16[2048,1000]{0,1:T(8,128)(2,1)} %param.18) | copy-start | bytes 12288004
  167.8 218.6 %all-gather.35.cloned.1.call-start = ((), (), s32[]{:S(2)}) async-start(), calls=%async_computation.8 | async-start | bytes 1081344 | tf_op jit(solution)/shard_map/all_gather | solution.py:43
  204.3 5.9 %copy-start.9 = (bf16[1,1536,2048]{2,1,0:T(8,128)(2,1)S(1)}, bf16[1,1536,2048]{2,1,0:T(8,128)(2,1)}, u32[]{:S(2)}) copy-start(bf16[1,1536,2048]{2,1,0:T(8,128)(2,1)} %all-gather.25.cloned.1.call-done) | copy-start | bytes 18874372
  204.4 6.0 %copy-start.14 = (bf16[2048,1000]{0,1:T(8,128)(2,1)S(1)}, bf16[2048,1000]{0,1:T(8,128)(2,1)}, u32[]{:S(2)}) copy-start(bf16[2048,1000]{0,1:T(8,128)(2,1)} %param.18) | copy-start | bytes 12288004
  217.7 212.9 %all-gather.33.cloned.1.call-start = ((), (), s32[]{:S(2)}) async-start(), calls=%async_computation.7 | async-start | bytes 1081344 | tf_op jit(solution)/shard_map/all_gather | solution.py:43
  254.2 5.9 %copy-start.8 = (bf16[1,1536,2048]{2,1,0:T(8,128)(2,1)S(1)}, bf16[1,1536,2048]{2,1,0:T(8,128)(2,1)}, u32[]{:S(2)}) copy-start(bf16[1,1536,2048]{2,1,0:T(8,128)(2,1)} %all-gather.23.cloned.1.call-done) | copy-start | bytes 18874372
  254.2 5.9 %copy-start.15 = (bf16[2048,1000]{0,1:T(8,128)(2,1)S(1)}, bf16[2048,1000]{0,1:T(8,128)(2,1)}, u32[]{:S(2)}) copy-start(bf16[2048,1000]{0,1:T(8,128)(2,1)} %param.18) | copy-start | bytes 12288004
  265.4 2.1 copy-start.16
  432.5 1.3 copy-start
  433.0 1.0 copy-start.1
  433.1 1.0 copy-start.2
  433.1 1.8 copy-start.3
  433.1 1.8 copy-start.5
  433.1 1.8 copy-start.6
  433.1 4.0 copy-start.4
  433.1 19.2 %copy-start.7 = (s32[16]{0:T(128)S(1)}, s32[16]{0:T(128)}, u32[]{:S(2)}) copy-start(s32[16]{0:T(128)} %param.21) | copy-start | bytes 196
  441.6 10.4 %collective-permute-start = (f32[4]{0:T(128)S(1)}, f32[4]{0:T(128)S(1)}, u32[]{:S(2)}, u32[]{:S(2)}) collective-permute-start(f32[4]{0:T(128)S(1)} %pad_maximum_fusion.2), channel_id=1, source_target_pairs={{0,32},{32,64},{64,96},{96,0},{1,33},{33,65},{65,97},{97,1},{2,34}... | collective-permute-start | bytes 56 | tf_op jit(solution)/shard_map/ppermute | solution.py:79
  443.2 9.0 %collective-permute-start.1 = (f32[4]{0:T(128)S(1)}, f32[4]{0:T(128)S(1)}, u32[]{:S(2)}, u32[]{:S(2)}) collective-permute-start(f32[4]{0:T(128)S(1)} %pad_maximum_fusion.2), channel_id=1, source_target_pairs={{0,64},{32,96},{64,0},{96,32},{1,65},{33,97},{65,1},{97,33},{2,66}... | collective-permute-start | bytes 56 | tf_op jit(solution)/shard_map/ppermute | solution.py:79
  446.0 6.2 %collective-permute-start.2 = (f32[4]{0:T(128)S(1)}, f32[4]{0:T(128)S(1)}, u32[]{:S(2)}, u32[]{:S(2)}) collective-permute-start(f32[4]{0:T(128)S(1)} %pad_maximum_fusion.2), channel_id=1, source_target_pairs={{0,96},{32,0},{64,32},{96,64},{1,97},{33,1},{65,33},{97,65},{2,98}... | collective-permute-start | bytes 56 | tf_op jit(solution)/shard_map/ppermute | solution.py:79
Sparse Core Ops, SparseCore 0:
  10.2 44.4 all-gather.26
  57.0 47.5 all-gather.20
  106.8 47.6 all-gather.18
  156.6 47.6 all-gather.24
  206.4 47.6 all-gather.22
  256.3 41.9 all-gather.30
  300.5 41.7 all-gather.28
  344.6 41.7 all-gather.34
  388.7 41.8 all-gather.32
